TPU v7x, 32 devices: a whole 2x2x4 slice. The times are simulated.
32 devices in a mesh: shots: 2 (over y), gx: 4 (over z), gy: 4 (over x, core).
Axes of the slice: x: 2, y: 2, z: 4, core: 2. Of those that a mesh axis runs over, the one named last changes fastest.
Arguments:
- p_now: float32 [64, 64, 128], P(('shots', 'gx'), 'gy'), parts along dimension 0, may hold values from -6 to 6
- q_now: float32 [64, 64, 128], P(('shots', 'gx'), 'gy'), parts along dimension 0, may hold values from -6 to 6
- p_prev: float32 [64, 64, 128], P(('shots', 'gx'), 'gy'), parts along dimension 0, may hold values from -6 to 6
- q_prev: float32 [64, 64, 128], P(('shots', 'gx'), 'gy'), parts along dimension 0, may hold values from -6 to 6
- speed: float32 [32, 64, 128], P('gx', 'gy'), may hold values from 0.05 to 0.2
- epsilon: float32 [32, 64, 128], P('gx', 'gy'), may hold values from 0.05 to 0.35
- delta: float32 [32, 64, 128], P('gx', 'gy'), may hold values from 0 to 0.3
- theta: float32 [32, 64, 128], P('gx', 'gy'), may hold values from -1 to 1
- phi: float32 [32, 64, 128], P('gx', 'gy'), may hold values from -3.140625 to 3.140625
- snapshots: bfloat16 [2, 64, 64, 128], P(None, ('shots', 'gx'), 'gy'), parts along dimension 1, may hold values from -6 to 6
- traces: float32 [1024, 4096], P(None, ('shots', 'gx', 'gy')), parts along dimension 1, may hold values from -6 to 6
- time_steps: int32 [4], P('shots'), parts along dimension 0, may hold values from 0 to 1023
- rec_owner: int32 [4096, 1], P(('shots', 'gx', 'gy')), parts along dimension 0, may hold values from 0 to 3; in each aligned block of 128 rows (0 to 127, 128 to 255, ...) at most 64 rows name the same one
- rec_local: int32 [4096], P(('shots', 'gx', 'gy')), parts along dimension 0, may hold values from 0 to 16383
Outputs:
- p_next: float32 [64, 64, 128], P(('shots', 'gx'), 'gy'), parts along dimension 0
- q_next: float32 [64, 64, 128], P(('shots', 'gx'), 'gy'), parts along dimension 0
- p_mid: float32 [64, 64, 128], P(('shots', 'gx'), 'gy'), parts along dimension 0
- q_mid: float32 [64, 64, 128], P(('shots', 'gx'), 'gy'), parts along dimension 0
- image: float32 [64, 64, 128], P(('shots', 'gx'), 'gy'), parts along dimension 0
There are 2 independent parts, one for each index of `shots`. A program takes and returns all parts, laid end to end along the dimension named above; an argument that names none is the same for every part. Nothing has to cross between parts.
Inputs may be any that keep to these rules, and one draw needn't show every extreme that they name: `rec_owner`: the 128 receivers of one device (aligned blocks of 128 rows) name any one owner at most 64 times, a bound that some block reaches. `rec_local`: A receiver's cell lies in the band of the second dimension that the device holding the receiver covers.
All inputs are finite; a program needn't handle non-finite values.
Results may differ from a plain program's by a relative error of at most 0.0003.
Values sent between devices are 32-bit elements; how exact they have to be, the bound alone decides.
No kernel may reach another device: no remote copies, remote signals or barrier semaphores. Data moves between devices by JAX's collectives and lax.ppermute only.
A program may use at most 64 MiB of HBM per device.

v0:
```python
import jax
import jax.numpy as jnp
from jax import lax
from jax.sharding import PartitionSpec as P

second_coef = (-205.0 / 72.0, 8.0 / 5.0, -1.0 / 5.0, 8.0 / 315.0, -1.0 / 560.0)
first_coef = (4.0 / 5.0, -1.0 / 5.0, 4.0 / 105.0, -1.0 / 280.0)


def padded_2(cells, sides, width):
    for axis, dim in sides:
        count = lax.axis_size(axis)
        ends = count - 1
        head = lax.slice_in_dim(cells, 0, width, axis=dim)
        tail = lax.slice_in_dim(cells, cells.shape[dim] - width, cells.shape[dim], axis=dim)
        cells = jnp.concatenate(
            [
                lax.ppermute(tail, axis, [(i, (i + 1) % count) for i in range(ends)]),
                cells,
                lax.ppermute(head, axis, [((i + 1) % count, i) for i in range(ends)]),
            ],
            axis=dim,
        )
    return cells


def derivatives(padded, sx, sy, sz):

    def part(dx, dy, dz):
        return padded[:, 4 + dx : 4 + dx + sx, 4 + dy : 4 + dy + sy, 4 + dz : 4 + dz + sz]

    centre = part(0, 0, 0)
    dxx = second_coef[0] * centre
    dyy = second_coef[0] * centre
    dzz = second_coef[0] * centre
    for k in range(1, 5):
        dxx = dxx + second_coef[k] * (part(k, 0, 0) + part(-k, 0, 0))
        dyy = dyy + second_coef[k] * (part(0, k, 0) + part(0, -k, 0))
        dzz = dzz + second_coef[k] * (part(0, 0, k) + part(0, 0, -k))
    dy_wide = 0.0
    dz_xwide = 0.0
    dz_ywide = 0.0
    for k in range(1, 5):
        weight = first_coef[k - 1]
        dy_wide = dy_wide + weight * (
            padded[:, :, 4 + k : 4 + k + sy, 4 : 4 + sz]
            - padded[:, :, 4 - k : 4 - k + sy, 4 : 4 + sz]
        )
        dz_xwide = dz_xwide + weight * (
            padded[:, :, 4 : 4 + sy, 4 + k : 4 + k + sz]
            - padded[:, :, 4 : 4 + sy, 4 - k : 4 - k + sz]
        )
        dz_ywide = dz_ywide + weight * (
            padded[:, 4 : 4 + sx, :, 4 + k : 4 + k + sz]
            - padded[:, 4 : 4 + sx, :, 4 - k : 4 - k + sz]
        )
    dxy = 0.0
    dxz = 0.0
    dyz = 0.0
    for k in range(1, 5):
        weight = first_coef[k - 1]
        dxy = dxy + weight * (dy_wide[:, 4 + k : 4 + k + sx] - dy_wide[:, 4 - k : 4 - k + sx])
        dxz = dxz + weight * (dz_xwide[:, 4 + k : 4 + k + sx] - dz_xwide[:, 4 - k : 4 - k + sx])
        dyz = dyz + weight * (
            dz_ywide[:, :, 4 + k : 4 + k + sy] - dz_ywide[:, :, 4 - k : 4 - k + sy]
        )
    return (centre, dxx, dyy, dzz, dxy, dxz, dyz)


def advance(padded, previous, speed, epsilon, delta, theta, phi, source):
    sx, sy, sz = (previous.shape[1], previous.shape[2], previous.shape[3])
    centre, dxx, dyy, dzz, dxy, dxz, dyz = derivatives(padded, sx, sy, sz)
    axis_x = jnp.sin(theta) * jnp.cos(phi)
    axis_y = jnp.sin(theta) * jnp.sin(phi)
    axis_z = jnp.cos(theta)
    rotated = (
        axis_x * axis_x * dxx
        + axis_y * axis_y * dyy
        + axis_z * axis_z * dzz
        + 2.0 * axis_x * axis_y * dxy
        + 2.0 * axis_x * axis_z * dxz
        + 2.0 * axis_y * axis_z * dyz
    )
    remainder = dxx + dyy + dzz - rotated
    root_delta = jnp.sqrt(1.0 + 2.0 * delta)
    p_new = (
        2.0 * centre[0]
        - previous[0]
        + speed * ((1.0 + 2.0 * epsilon) * remainder[0] + root_delta * rotated[1])
        + source
    )
    q_new = (
        2.0 * centre[1] - previous[1] + speed * (root_delta * remainder[0] + rotated[1]) + source
    )
    return jnp.stack([p_new, q_new])


def pad_depth(fields):
    return jnp.pad(fields, ((0, 0), (0, 0), (0, 0), (4, 4)))


def widened(fields):
    return pad_depth(padded_2(fields, (("gx", 1), ("gy", 2)), 4))


def local(
    p_now,
    q_now,
    p_prev,
    q_prev,
    speed,
    epsilon,
    delta,
    theta,
    phi,
    snapshots,
    traces,
    time_steps,
    rec_owner,
    rec_local,
):
    sx, sy, sz = p_now.shape
    cells = sx * sy * sz
    groups = lax.axis_size("gx")
    held = rec_local.shape[0]
    samples = jnp.take(traces, time_steps, axis=0)
    owner = rec_owner[:, 0]
    capacity = 2 * held // groups
    onehot = (owner[:, None] == jnp.arange(groups, dtype=jnp.int32)[None, :]).astype(jnp.int32)
    running = jnp.cumsum(onehot, axis=0)
    rank = jnp.sum(onehot * running, axis=1) - 1
    position = owner * capacity + rank
    payload = jnp.concatenate([samples, rec_local.astype(jnp.float32)[None, :]], axis=0)
    slots = jnp.zeros((3, groups * capacity), jnp.float32).at[:, position].set(payload)
    slots = slots.reshape(3, groups, capacity)
    arrived = lax.all_to_all(slots, "gx", split_axis=1, concat_axis=1, tiled=True)
    values = arrived[0:2].reshape(2, groups * capacity)
    target = arrived[2].reshape(groups * capacity).astype(jnp.int32)
    sources = jnp.zeros((2, cells), jnp.float32).at[:, target].add(values).reshape(2, sx, sy, sz)
    current = jnp.stack([p_now, q_now])
    earlier = jnp.stack([p_prev, q_prev])
    middle = advance(widened(current), earlier, speed, epsilon, delta, theta, phi, sources[0])
    final = advance(widened(middle), current, speed, epsilon, delta, theta, phi, sources[1])
    image = (
        snapshots[0].astype(jnp.float32) * middle[0] + snapshots[1].astype(jnp.float32) * final[0]
    )
    return (final[0], final[1], middle[0], middle[1], image)


def solution(mesh):
    return jax.shard_map(
        local,
        mesh=mesh,
        in_specs=(
            P(("shots", "gx"), "gy", None),
            P(("shots", "gx"), "gy", None),
            P(("shots", "gx"), "gy", None),
            P(("shots", "gx"), "gy", None),
            P("gx", "gy", None),
            P("gx", "gy", None),
            P("gx", "gy", None),
            P("gx", "gy", None),
            P("gx", "gy", None),
            P(None, ("shots", "gx"), "gy", None),
            P(None, ("shots", "gx", "gy")),
            P("shots"),
            P(("shots", "gx", "gy"), None),
            P(("shots", "gx", "gy")),
        ),
        out_specs=(
            P(("shots", "gx"), "gy", None),
            P(("shots", "gx"), "gy", None),
            P(("shots", "gx"), "gy", None),
            P(("shots", "gx"), "gy", None),
            P(("shots", "gx"), "gy", None),
        ),
        check_vma=False,
    )
```

profile of v0, /device:TPU:18, one launch (start us, length us, event | category | flops | bytes accessed | tf_op | source)
XLA Modules:
  0.0 71.5 jit_solution(5272176775762559091)
XLA Ops:
  0.6 0.7 %compare_select_fusion.1 = s32[2]{0:T(128)S(1)} fusion(s32[2]{0:T(128)} %param.25), kind=kLoop, calls=%fused_computation.299 | loop fusion | flops 6 | bytes 16 | tf_op jit(solution)/shard_map/jit(_take)/jit(_where)/select_n | solution.py:126
  1.4 0.7 compare_and_fusion
  2.0 0.7 %fusion.156 = s32[128,4]{1,0:T(8,128)S(1)} fusion(s32[128]{0:T(128)} %bitcast.80), kind=kLoop, calls=%fused_computation.286 | loop fusion | flops 1024 | bytes 2560 | tf_op jit(solution)/shard_map/convert_element_type | solution.py:129
  2.9 0.8 %select_reduce_fusion = s32[128]{0:T(128)S(1)} fusion(s32[128,4]{1,0:T(8,128)S(1)} %reduce_window_sum.11, s32[128]{0:T(128)} %bitcast.81), kind=kLoop, calls=%fused_computation.284 | loop fusion | flops 1408 | bytes 3072 | tf_op jit(solution)/shard_map/reduce_sum | solution.py:131
  3.8 0.7 fusion.160
  4.4 0.7 convert_bitcast_fusion
  5.1 0.6 gather_fusion
  5.9 0.9 %scatter_custom_fusion = f32[3,256]{0,1:T(8,128)S(1)} fusion(s32[128]{0:T(128)S(1)} %fusion.160, f32[128,3]{1,0:T(8,128)S(1)} %copy.25, f32[]{:T(128)} %constant.26.clone.1), kind=kCustom, calls=%fused_computation.287 | custom fusion | bytes 3076 | tf_op jit(solution)/shard_map/scatter | solution.py:134
  6.9 0.7 reshape.111
  7.6 5.2 %all-to-all-start = ((f32[4,1,192]{2,1,0:T(1,128)}), f32[4,1,192]{2,1,0:T(1,128)S(1)}, u32[]{:S(2)}, u32[]{:S(2)}) async-start(f32[4,1,192]{2,1,0:T(1,128)} %reshape.111), calls=%async_computation | async-start | bytes 8192 | tf_op jit(solution)/shard_map/all_to_all | solution.py:136
  12.8 0.8 %fusion.152 = (f32[2,4,16,128]{3,2,1,0:T(8,128)S(1)}, f32[2,4,16,128]{3,2,1,0:T(8,128)S(1)}) fusion(f32[1,8,16,128]{3,2,1,0:T(8,128)} %bitcast.59, f32[1,8,16,128]{3,2,1,0:T(8,128)} %bitcast.47), kind=kLoop, calls=%fused_computation.259 | loop fusion | flops 32768 | bytes 262144 | tf_op jit(solution)/shard_map/stack | solution.py:140
  13.6 2.5 %collective-permute-start = (f32[2,4,16,128]{3,2,1,0:T(8,128)S(1)}, f32[2,4,16,128]{3,2,1,0:T(8,128)S(1)}, u32[]{:S(2)}, u32[]{:S(2)}) collective-permute-start(f32[2,4,16,128]{3,2,1,0:T(8,128)S(1)} %get-tuple-element.42), channel_id=1, source_target_pairs={{4,0},{8,4},{12,8},{5,1},{9,5},{13,9},{6,2},{10,6},{14,10},{7,3},{... | collective-permute-start | bytes 196616 | tf_op jit(solution)/shard_map/ppermute | solution.py:20
  16.1 3.4 %collective-permute-start.1 = (f32[2,4,16,128]{3,2,1,0:T(8,128)S(1)}, f32[2,4,16,128]{3,2,1,0:T(8,128)S(1)}, u32[]{:S(2)}, u32[]{:S(2)}) collective-permute-start(f32[2,4,16,128]{3,2,1,0:T(8,128)S(1)} %get-tuple-element.41), channel_id=1, source_target_pairs={{0,4},{4,8},{8,12},{1,5},{5,9},{9,13},{2,6},{6,10},{10,14},{3,7},{... | collective-permute-start | bytes 196616 | tf_op jit(solution)/shard_map/ppermute | solution.py:18
  19.4 1.1 %fusion.171 = (f32[8,16,128]{2,1,0:T(8,128)S(1)}, f32[8,16,128]{2,1,0:T(8,128)S(1)}) fusion(f32[8,16,128]{2,1,0:T(8,128)} %param.21), kind=kLoop, calls=%fused_computation.311 | loop fusion | bytes 196608 | tf_op jit(solution)/shard_map/sin | solution.py:73
  20.5 1.1 %fusion.161 = (f32[8,16,128]{2,1,0:T(8,128)S(1)}, f32[8,16,128]{2,1,0:T(8,128)S(1)}, f32[8,16,128]{2,1,0:T(8,128)S(1)}, f32[8,16,128]{2,1,0:T(8,128)S(1)}, f32[8...) fusion(f32[8,16,128]{2,1,0:T(8,128)S(1)} %get-tuple-element.44, f32[8,16,128]{2,1,0:T(8,128)} %param.22, ...), kind=kLoop, calls=%fused_computation.309 | loop fusion | flops 163840 | bytes 589824 | tf_op jit(solution)/shard_map/mul | solution.py:77
  22.2 0.7 reduce.8
  23.3 5.1 %scatter_custom_fusion.1 = f32[2,16384]{0,1:T(8,128)} fusion(s32[256]{0:T(256)S(1)} %bitcast.82, f32[256,2]{1,0:T(8,128)S(1)} %copy.28, f32[]{:T(128)} %constant.26.clone.1), kind=kCustom, calls=%fused_computation.5 | custom fusion | flops 512 | bytes 131076 | tf_op jit(solution)/shard_map/scatter-add | solution.py:139
  28.4 12.3 %slice_reduce_fusion.1 = (f32[16384]{0:T(1024)S(1)}, f32[16384]{0:T(1024)S(1)}) fusion(f32[2,16384]{0,1:T(8,128)} %scatter_custom_fusion.1), kind=kLoop, calls=%fused_computation.4 | loop fusion | bytes 262144 | tf_op jit(solution)/shard_map/slice | solution.py:142
  40.8 1.9 %collective-permute-start.2 = (f32[2,16,4,128]{3,2,1,0:T(4,128)S(1)}, f32[2,16,4,128]{3,2,1,0:T(4,128)S(1)}, u32[]{:S(2)}, u32[]{:S(2)}) collective-permute-start(f32[2,16,4,128]{3,2,1,0:T(4,128)S(1)} %get-tuple-element.27), channel_id=1, source_target_pairs={{1,0},{2,1},{3,2},{5,4},{6,5},{7,6},{9,8},{10,9},{11,10},{13,12},{... | collective-permute-start | bytes 196616 | tf_op jit(solution)/shard_map/ppermute | solution.py:20
  42.8 2.5 %collective-permute-start.3 = (f32[2,16,4,128]{3,2,1,0:T(4,128)S(1)}, f32[2,16,4,128]{3,2,1,0:T(4,128)S(1)}, u32[]{:S(2)}, u32[]{:S(2)}) collective-permute-start(f32[2,16,4,128]{3,2,1,0:T(4,128)S(1)} %get-tuple-element.26), channel_id=1, source_target_pairs={{0,1},{1,2},{2,3},{4,5},{5,6},{6,7},{8,9},{9,10},{10,11},{12,13},{... | collective-permute-start | bytes 196616 | tf_op jit(solution)/shard_map/ppermute | solution.py:18
  45.4 3.1 %collective-permute-done.3 = f32[2,16,4,128]{3,2,1,0:T(4,128)S(1)} collective-permute-done((f32[2,16,4,128]{3,2,1,0:T(4,128)S(1)}, f32[2,16,4,128]{3,2,1,0:T(4,128)S(1)}, u32[]{:S(2)}, u32[]{:S(2)}) %collective-permute-start.3) | collective-permute-done | bytes 65568 | tf_op jit(solution)/shard_map/ppermute | solution.py:18
  49.4 0.7 fusion.18
  50.1 0.6 fusion.101
  50.9 3.1 %collective-permute-start.4 = (f32[2,4,16,128]{3,2,1,0:T(8,128)S(1)}, f32[2,4,16,128]{3,2,1,0:T(8,128)S(1)}, u32[]{:S(2)}, u32[]{:S(2)}) collective-permute-start(f32[2,4,16,128]{3,2,1,0:T(8,128)S(1)} %get-tuple-element.33), channel_id=1, source_target_pairs={{4,0},{8,4},{12,8},{5,1},{9,5},{13,9},{6,2},{10,6},{14,10},{7,3},{... | collective-permute-start | bytes 196616 | tf_op jit(solution)/shard_map/ppermute | solution.py:20
  54.0 2.7 %collective-permute-start.5 = (f32[2,4,16,128]{3,2,1,0:T(8,128)S(1)}, f32[2,4,16,128]{3,2,1,0:T(8,128)S(1)}, u32[]{:S(2)}, u32[]{:S(2)}) collective-permute-start(f32[2,4,16,128]{3,2,1,0:T(8,128)S(1)} %get-tuple-element.32), channel_id=1, source_target_pairs={{0,4},{4,8},{8,12},{1,5},{5,9},{9,13},{2,6},{6,10},{10,14},{3,7},{... | collective-permute-start | bytes 196616 | tf_op jit(solution)/shard_map/ppermute | solution.py:18
  57.0 3.1 %collective-permute-done.5 = f32[2,4,16,128]{3,2,1,0:T(8,128)S(1)} collective-permute-done((f32[2,4,16,128]{3,2,1,0:T(8,128)S(1)}, f32[2,4,16,128]{3,2,1,0:T(8,128)S(1)}, u32[]{:S(2)}, u32[]{:S(2)}) %collective-permute-start.5) | collective-permute-done | bytes 65568 | tf_op jit(solution)/shard_map/ppermute | solution.py:18
  60.2 1.9 %collective-permute-start.6 = (f32[2,16,4,128]{3,2,1,0:T(4,128)S(1)}, f32[2,16,4,128]{3,2,1,0:T(4,128)S(1)}, u32[]{:S(2)}, u32[]{:S(2)}) collective-permute-start(f32[2,16,4,128]{3,2,1,0:T(4,128)S(1)} %get-tuple-element.23), channel_id=1, source_target_pairs={{1,0},{2,1},{3,2},{5,4},{6,5},{7,6},{9,8},{10,9},{11,10},{13,12},{... | collective-permute-start | bytes 196616 | tf_op jit(solution)/shard_map/ppermute | solution.py:20
  62.1 2.5 %collective-permute-start.7 = (f32[2,16,4,128]{3,2,1,0:T(4,128)S(1)}, f32[2,16,4,128]{3,2,1,0:T(4,128)S(1)}, u32[]{:S(2)}, u32[]{:S(2)}) collective-permute-start(f32[2,16,4,128]{3,2,1,0:T(4,128)S(1)} %get-tuple-element.22), channel_id=1, source_target_pairs={{0,1},{1,2},{2,3},{4,5},{5,6},{6,7},{8,9},{9,10},{10,11},{12,13},{... | collective-permute-start | bytes 196616 | tf_op jit(solution)/shard_map/ppermute | solution.py:18
  64.7 3.1 %collective-permute-done.7 = f32[2,16,4,128]{3,2,1,0:T(4,128)S(1)} collective-permute-done((f32[2,16,4,128]{3,2,1,0:T(4,128)S(1)}, f32[2,16,4,128]{3,2,1,0:T(4,128)S(1)}, u32[]{:S(2)}, u32[]{:S(2)}) %collective-permute-start.7) | collective-permute-done | bytes 65568 | tf_op jit(solution)/shard_map/ppermute | solution.py:18
  69.5 0.6 fusion.50
  70.1 0.7 %fusion.155 = (f32[8,16,128]{2,1,0:T(8,128)}, f32[8,16,128]{2,1,0:T(8,128)}, f32[8,16,128]{2,1,0:T(8,128)S(1)}) fusion(f32[8,16,128]{2,1,0:T(8,128)S(1)} %add_add_fusion.3, bf16[2,8,16,128]{3,2,1,0:T(8,128)(2,1)S(1)} %copy-done.10, f32[8,16,128]{2,1,0:T(8,128)S(1)} %bitcast.73, f32[8,16,128]{2,1,0:T(8,128)S(1)} %copy-done.5, ...), kind=kLoop, calls=%fused_computation.279 | loop fusion | flops 327680 | bytes 983040 | tf_op jit(solution)/shard_map/add | solution.py:145
  70.8 0.7 add_add_fusion
  (58 shorter events, 4.6 us)
Async XLA Ops:
  0.6 4.5 %copy-start = (f32[1024,128]{1,0:T(8,128)S(1)}, f32[1024,128]{1,0:T(8,128)}, u32[]{:S(2)}) copy-start(f32[1024,128]{1,0:T(8,128)} %param.24) | copy-start | bytes 1572868
  7.6 14.1 %all-to-all-start = ((f32[4,1,192]{2,1,0:T(1,128)}), f32[4,1,192]{2,1,0:T(1,128)S(1)}, u32[]{:S(2)}, u32[]{:S(2)}) async-start(f32[4,1,192]{2,1,0:T(1,128)} %reshape.111), calls=%async_computation | async-start | bytes 8192 | tf_op jit(solution)/shard_map/all_to_all | solution.py:136
  13.6 27.1 %collective-permute-start = (f32[2,4,16,128]{3,2,1,0:T(8,128)S(1)}, f32[2,4,16,128]{3,2,1,0:T(8,128)S(1)}, u32[]{:S(2)}, u32[]{:S(2)}) collective-permute-start(f32[2,4,16,128]{3,2,1,0:T(8,128)S(1)} %get-tuple-element.42), channel_id=1, source_target_pairs={{4,0},{8,4},{12,8},{5,1},{9,5},{13,9},{6,2},{10,6},{14,10},{7,3},{... | collective-permute-start | bytes 196616 | tf_op jit(solution)/shard_map/ppermute | solution.py:20
  16.1 24.7 %collective-permute-start.1 = (f32[2,4,16,128]{3,2,1,0:T(8,128)S(1)}, f32[2,4,16,128]{3,2,1,0:T(8,128)S(1)}, u32[]{:S(2)}, u32[]{:S(2)}) collective-permute-start(f32[2,4,16,128]{3,2,1,0:T(8,128)S(1)} %get-tuple-element.41), channel_id=1, source_target_pairs={{0,4},{4,8},{8,12},{1,5},{5,9},{9,13},{2,6},{6,10},{10,14},{3,7},{... | collective-permute-start | bytes 196616 | tf_op jit(solution)/shard_map/ppermute | solution.py:18
  28.4 12.3 %copy-start.1 = (f32[8,16,128]{2,1,0:T(8,128)S(1)}, f32[8,16,128]{2,1,0:T(8,128)}, u32[]{:S(2)}) copy-start(f32[8,16,128]{2,1,0:T(8,128)} %param.15) | copy-start | bytes 196612
  28.4 12.3 %copy-start.3 = (f32[8,16,128]{2,1,0:T(8,128)S(1)}, f32[8,16,128]{2,1,0:T(8,128)}, u32[]{:S(2)}) copy-start(f32[8,16,128]{2,1,0:T(8,128)} %param.14) | copy-start | bytes 196612
  40.8 4.6 %collective-permute-start.2 = (f32[2,16,4,128]{3,2,1,0:T(4,128)S(1)}, f32[2,16,4,128]{3,2,1,0:T(4,128)S(1)}, u32[]{:S(2)}, u32[]{:S(2)}) collective-permute-start(f32[2,16,4,128]{3,2,1,0:T(4,128)S(1)} %get-tuple-element.27), channel_id=1, source_target_pairs={{1,0},{2,1},{3,2},{5,4},{6,5},{7,6},{9,8},{10,9},{11,10},{13,12},{... | collective-permute-start | bytes 196616 | tf_op jit(solution)/shard_map/ppermute | solution.py:20
  42.7 7.9 %copy-start.5 = (f32[8,16,128]{2,1,0:T(8,128)S(1)}, f32[8,16,128]{2,1,0:T(8,128)}, u32[]{:S(2)}) copy-start(f32[8,16,128]{2,1,0:T(8,128)} %param.18) | copy-start | bytes 196612
  42.7 7.9 %copy-start.6 = (f32[8,16,128]{2,1,0:T(8,128)S(1)}, f32[8,16,128]{2,1,0:T(8,128)}, u32[]{:S(2)}) copy-start(f32[8,16,128]{2,1,0:T(8,128)} %param.20) | copy-start | bytes 196612
  42.7 7.9 %copy-start.8 = (f32[8,16,128]{2,1,0:T(8,128)S(1)}, f32[8,16,128]{2,1,0:T(8,128)}, u32[]{:S(2)}) copy-start(f32[8,16,128]{2,1,0:T(8,128)} %param.17) | copy-start | bytes 196612
  42.8 5.7 %collective-permute-start.3 = (f32[2,16,4,128]{3,2,1,0:T(4,128)S(1)}, f32[2,16,4,128]{3,2,1,0:T(4,128)S(1)}, u32[]{:S(2)}, u32[]{:S(2)}) collective-permute-start(f32[2,16,4,128]{3,2,1,0:T(4,128)S(1)} %get-tuple-element.26), channel_id=1, source_target_pairs={{0,1},{1,2},{2,3},{4,5},{5,6},{6,7},{8,9},{9,10},{10,11},{12,13},{... | collective-permute-start | bytes 196616 | tf_op jit(solution)/shard_map/ppermute | solution.py:18
  45.3 5.4 %copy-start.7 = (f32[8,16,128]{2,1,0:T(8,128)S(1)}, f32[8,16,128]{2,1,0:T(8,128)}, u32[]{:S(2)}) copy-start(f32[8,16,128]{2,1,0:T(8,128)} %param.19) | copy-start | bytes 196612
  45.4 5.4 %copy-start.9 = (f32[8,16,128]{2,1,0:T(8,128)S(1)}, f32[8,16,128]{2,1,0:T(8,128)}, u32[]{:S(2)}) copy-start(f32[8,16,128]{2,1,0:T(8,128)} %param.16) | copy-start | bytes 196612
  50.7 20.1 %copy-start.2 = (f32[8,16,128]{2,1,0:T(8,128)}, f32[8,16,128]{2,1,0:T(8,128)S(1)}, u32[]{:S(2)}) copy-start(f32[8,16,128]{2,1,0:T(8,128)S(1)} %get-tuple-element.14) | copy-start | bytes 196612
  50.8 19.2 %copy-start.4 = (f32[8,16,128]{2,1,0:T(8,128)}, f32[8,16,128]{2,1,0:T(8,128)S(1)}, u32[]{:S(2)}) copy-start(f32[8,16,128]{2,1,0:T(8,128)S(1)} %add_add_fusion.3) | copy-start | bytes 196612
  50.9 6.2 %collective-permute-start.4 = (f32[2,4,16,128]{3,2,1,0:T(8,128)S(1)}, f32[2,4,16,128]{3,2,1,0:T(8,128)S(1)}, u32[]{:S(2)}, u32[]{:S(2)}) collective-permute-start(f32[2,4,16,128]{3,2,1,0:T(8,128)S(1)} %get-tuple-element.33), channel_id=1, source_target_pairs={{4,0},{8,4},{12,8},{5,1},{9,5},{13,9},{6,2},{10,6},{14,10},{7,3},{... | collective-permute-start | bytes 196616 | tf_op jit(solution)/shard_map/ppermute | solution.py:20
  54.0 6.2 %collective-permute-start.5 = (f32[2,4,16,128]{3,2,1,0:T(8,128)S(1)}, f32[2,4,16,128]{3,2,1,0:T(8,128)S(1)}, u32[]{:S(2)}, u32[]{:S(2)}) collective-permute-start(f32[2,4,16,128]{3,2,1,0:T(8,128)S(1)} %get-tuple-element.32), channel_id=1, source_target_pairs={{0,4},{4,8},{8,12},{1,5},{5,9},{9,13},{2,6},{6,10},{10,14},{3,7},{... | collective-permute-start | bytes 196616 | tf_op jit(solution)/shard_map/ppermute | solution.py:18
  60.2 4.5 %collective-permute-start.6 = (f32[2,16,4,128]{3,2,1,0:T(4,128)S(1)}, f32[2,16,4,128]{3,2,1,0:T(4,128)S(1)}, u32[]{:S(2)}, u32[]{:S(2)}) collective-permute-start(f32[2,16,4,128]{3,2,1,0:T(4,128)S(1)} %get-tuple-element.23), channel_id=1, source_target_pairs={{1,0},{2,1},{3,2},{5,4},{6,5},{7,6},{9,8},{10,9},{11,10},{13,12},{... | collective-permute-start | bytes 196616 | tf_op jit(solution)/shard_map/ppermute | solution.py:20
  62.1 8.0 %copy-start.10 = (bf16[2,8,16,128]{3,2,1,0:T(8,128)(2,1)S(1)}, bf16[2,8,16,128]{3,2,1,0:T(8,128)(2,1)}, u32[]{:S(2)}) copy-start(bf16[2,8,16,128]{3,2,1,0:T(8,128)(2,1)} %param.23) | copy-start | bytes 196612
  62.1 5.7 %collective-permute-start.7 = (f32[2,16,4,128]{3,2,1,0:T(4,128)S(1)}, f32[2,16,4,128]{3,2,1,0:T(4,128)S(1)}, u32[]{:S(2)}, u32[]{:S(2)}) collective-permute-start(f32[2,16,4,128]{3,2,1,0:T(4,128)S(1)} %get-tuple-element.22), channel_id=1, source_target_pairs={{0,1},{1,2},{2,3},{4,5},{5,6},{6,7},{8,9},{9,10},{10,11},{12,13},{... | collective-permute-start | bytes 196616 | tf_op jit(solution)/shard_map/ppermute | solution.py:18
where the time goes:
time: 72.1 us; the launch traced here: 71.5 us
  starting transfers between devices  25.8 us (36%)
  other arithmetic  18.3 us (25%)
  local copies, waits for them, and re-layouts  16.7 us (23%)
  waiting for transfers between devices  9.66 us (13%)
  between operations  1.04 us (1%)
    slice x1, local copies, waits for them, and re-layouts, local(): sources[0]  12.3 us
    ppermute x4, starting transfers between devices, padded_2(): lax.ppermute(tail, axis, [(i, (i + 1) % count) for i in range(ends)])  11.2 us
    ppermute x4, starting transfers between devices, padded_2(): lax.ppermute(head, axis, [((i + 1) % count, i) for i in range(ends)])  9.42 us
    ppermute x4, waiting for transfers between devices, padded_2(): lax.ppermute(tail, axis, [(i, (i + 1) % count) for i in range(ends)])  9.35 us
    all_to_all x1, starting transfers between devices, local(): lax.all_to_all(slots, 'gx', split_axis=1, concat_axis=1, tiled=True)  5.2 us
    scatter-add x1, other arithmetic, local(): jnp.zeros((2, cells), jnp.float32).at[:, target].add(values)  5.14 us
  transfers between devices with their start and end apart: 9, of which 4 were waited for; matrix products, arithmetic and copies ran while one was open for 31% of the time, Pallas kernels for 0%

commit v1 on v0

--- a/solution.py
+++ b/solution.py
@@ -133,7 +133,10 @@
     payload = jnp.concatenate([samples, rec_local.astype(jnp.float32)[None, :]], axis=0)
     slots = jnp.zeros((3, groups * capacity), jnp.float32).at[:, position].set(payload)
     slots = slots.reshape(3, groups, capacity)
-    arrived = lax.all_to_all(slots, "gx", split_axis=1, concat_axis=1, tiled=True)
+    size = lax.axis_size("gx")
+    pieces = jnp.stack(jnp.split(slots, size, axis=1), axis=0)
+    pieces = lax.all_to_all(pieces, "gx", split_axis=0, concat_axis=0)
+    arrived = jnp.concatenate(pieces, axis=1)
     values = arrived[0:2].reshape(2, groups * capacity)
     target = arrived[2].reshape(groups * capacity).astype(jnp.int32)
     sources = jnp.zeros((2, cells), jnp.float32).at[:, target].add(values).reshape(2, sx, sy, sz)

time: 72.1 us -> 73.1 us (1.014)
  transfers between devices with their start and end apart: 9 -> 9, of which waited for: 4 -> 4; matrix products, arithmetic and copies ran while one was open for 31% -> 30% of each run, Pallas kernels for 0% -> 0%
where the time goes in v1:
time: 73.1 us; the launch traced here: 72.4 us
  starting transfers between devices  25.8 us (35%)
  other arithmetic  19 us (26%)
  local copies, waits for them, and re-layouts  16.9 us (23%)
  waiting for transfers between devices  9.66 us (13%)
  between operations  1.06 us (1%)
    slice x1, local copies, waits for them, and re-layouts, local(): sources[0]  12.3 us
    ppermute x4, starting transfers between devices, padded_2(): lax.ppermute(tail, axis, [(i, (i + 1) % count) for i in range(ends)])  11.2 us
    ppermute x4, starting transfers between devices, padded_2(): lax.ppermute(head, axis, [((i + 1) % count, i) for i in range(ends)])  9.42 us
    ppermute x4, waiting for transfers between devices, padded_2(): lax.ppermute(tail, axis, [(i, (i + 1) % count) for i in range(ends)])  9.35 us
    all_to_all x1, starting transfers between devices, local(): pieces = lax.all_to_all(pieces, 'gx', split_axis=0, concat_axis=0)  5.2 us
    scatter-add x1, other arithmetic, local(): jnp.zeros((2, cells), jnp.float32).at[:, target].add(values)  5.13 us
  transfers between devices with their start and end apart: 9, of which 4 were waited for; matrix products, arithmetic and copies ran while one was open for 30% of the time, Pallas kernels for 0%

profile of v1, /device:TPU:18, one launch (start us, length us, event | category | flops | bytes accessed | tf_op | source)
XLA Modules:
  0.0 72.4 jit_solution(6660000155977564365)
XLA Ops:
  0.6 0.7 compare_select_fusion.1
  1.4 0.7 compare_and_fusion
  2.0 0.7 %fusion.156 = s32[128,4]{1,0:T(8,128)S(1)} fusion(s32[128]{0:T(128)} %bitcast.88), kind=kLoop, calls=%fused_computation.286 | loop fusion | flops 1024 | bytes 2560 | tf_op jit(solution)/shard_map/convert_element_type | solution.py:129
  2.9 0.8 %select_reduce_fusion = s32[128]{0:T(128)S(1)} fusion(s32[128,4]{1,0:T(8,128)S(1)} %reduce_window_sum.11, s32[128]{0:T(128)} %bitcast.89), kind=kLoop, calls=%fused_computation.284 | loop fusion | flops 1408 | bytes 3072 | tf_op jit(solution)/shard_map/reduce_sum | solution.py:131
  3.8 0.7 fusion.160
  4.4 0.7 convert_bitcast_fusion
  5.9 0.9 %scatter_custom_fusion = f32[3,256]{0,1:T(8,128)S(1)} fusion(s32[128]{0:T(128)S(1)} %fusion.160, f32[128,3]{1,0:T(8,128)S(1)} %copy.31, f32[]{:T(128)} %constant.26.clone.1), kind=kCustom, calls=%fused_computation.287 | custom fusion | bytes 3076 | tf_op jit(solution)/shard_map/scatter | solution.py:134
  7.7 0.7 reduce.8
  8.3 0.7 reshape.120
  9.0 5.2 %all-to-all-start = ((f32[4,1,192]{2,1,0:T(1,128)}), f32[4,1,192]{2,1,0:T(1,128)S(1)}, u32[]{:S(2)}, u32[]{:S(2)}) async-start(f32[4,1,192]{2,1,0:T(1,128)} %reshape.120), calls=%async_computation | async-start | bytes 8192 | tf_op jit(solution)/shard_map/all_to_all | solution.py:138
  14.2 0.8 %fusion.152 = (f32[2,4,16,128]{3,2,1,0:T(8,128)S(1)}, f32[2,4,16,128]{3,2,1,0:T(8,128)S(1)}) fusion(f32[1,8,16,128]{3,2,1,0:T(8,128)} %bitcast.64, f32[1,8,16,128]{3,2,1,0:T(8,128)} %bitcast.52), kind=kLoop, calls=%fused_computation.259 | loop fusion | flops 32768 | bytes 262144 | tf_op jit(solution)/shard_map/stack | solution.py:143
  15.0 2.5 %collective-permute-start = (f32[2,4,16,128]{3,2,1,0:T(8,128)S(1)}, f32[2,4,16,128]{3,2,1,0:T(8,128)S(1)}, u32[]{:S(2)}, u32[]{:S(2)}) collective-permute-start(f32[2,4,16,128]{3,2,1,0:T(8,128)S(1)} %get-tuple-element.42), channel_id=1, source_target_pairs={{4,0},{8,4},{12,8},{5,1},{9,5},{13,9},{6,2},{10,6},{14,10},{7,3},{... | collective-permute-start | bytes 196616 | tf_op jit(solution)/shard_map/ppermute | solution.py:20
  17.5 3.4 %collective-permute-start.1 = (f32[2,4,16,128]{3,2,1,0:T(8,128)S(1)}, f32[2,4,16,128]{3,2,1,0:T(8,128)S(1)}, u32[]{:S(2)}, u32[]{:S(2)}) collective-permute-start(f32[2,4,16,128]{3,2,1,0:T(8,128)S(1)} %get-tuple-element.41), channel_id=1, source_target_pairs={{0,4},{4,8},{8,12},{1,5},{5,9},{9,13},{2,6},{6,10},{10,14},{3,7},{... | collective-permute-start | bytes 196616 | tf_op jit(solution)/shard_map/ppermute | solution.py:18
  20.9 1.1 %fusion.172 = (f32[8,16,128]{2,1,0:T(8,128)S(1)}, f32[8,16,128]{2,1,0:T(8,128)S(1)}) fusion(f32[8,16,128]{2,1,0:T(8,128)} %param.21), kind=kLoop, calls=%fused_computation.313 | loop fusion | bytes 196608 | tf_op jit(solution)/shard_map/sin | solution.py:73
  22.0 1.1 %fusion.161 = (f32[8,16,128]{2,1,0:T(8,128)S(1)}, f32[8,16,128]{2,1,0:T(8,128)S(1)}, f32[8,16,128]{2,1,0:T(8,128)S(1)}, f32[8,16,128]{2,1,0:T(8,128)S(1)}, f32[8...) fusion(f32[8,16,128]{2,1,0:T(8,128)S(1)} %get-tuple-element.48, f32[8,16,128]{2,1,0:T(8,128)} %param.22, ...), kind=kLoop, calls=%fused_computation.310 | loop fusion | flops 163840 | bytes 589824 | tf_op jit(solution)/shard_map/mul | solution.py:77
  23.1 0.7 reduce.9
  24.2 5.1 %scatter_custom_fusion.1 = f32[2,16384]{0,1:T(8,128)} fusion(s32[256]{0:T(256)S(1)} %bitcast.90, f32[256,2]{1,0:T(8,128)S(1)} %copy.37, f32[]{:T(128)} %constant.26.clone.1), kind=kCustom, calls=%fused_computation.5 | custom fusion | flops 512 | bytes 131076 | tf_op jit(solution)/shard_map/scatter-add | solution.py:142
  29.3 12.3 %slice_reduce_fusion.1 = (f32[16384]{0:T(1024)S(1)}, f32[16384]{0:T(1024)S(1)}) fusion(f32[2,16384]{0,1:T(8,128)} %scatter_custom_fusion.1), kind=kLoop, calls=%fused_computation.4 | loop fusion | bytes 262144 | tf_op jit(solution)/shard_map/slice | solution.py:145
  41.7 1.9 %collective-permute-start.2 = (f32[2,16,4,128]{3,2,1,0:T(4,128)S(1)}, f32[2,16,4,128]{3,2,1,0:T(4,128)S(1)}, u32[]{:S(2)}, u32[]{:S(2)}) collective-permute-start(f32[2,16,4,128]{3,2,1,0:T(4,128)S(1)} %get-tuple-element.27), channel_id=1, source_target_pairs={{1,0},{2,1},{3,2},{5,4},{6,5},{7,6},{9,8},{10,9},{11,10},{13,12},{... | collective-permute-start | bytes 196616 | tf_op jit(solution)/shard_map/ppermute | solution.py:20
  43.7 2.5 %collective-permute-start.3 = (f32[2,16,4,128]{3,2,1,0:T(4,128)S(1)}, f32[2,16,4,128]{3,2,1,0:T(4,128)S(1)}, u32[]{:S(2)}, u32[]{:S(2)}) collective-permute-start(f32[2,16,4,128]{3,2,1,0:T(4,128)S(1)} %get-tuple-element.26), channel_id=1, source_target_pairs={{0,1},{1,2},{2,3},{4,5},{5,6},{6,7},{8,9},{9,10},{10,11},{12,13},{... | collective-permute-start | bytes 196616 | tf_op jit(solution)/shard_map/ppermute | solution.py:18
  46.3 3.1 %collective-permute-done.3 = f32[2,16,4,128]{3,2,1,0:T(4,128)S(1)} collective-permute-done((f32[2,16,4,128]{3,2,1,0:T(4,128)S(1)}, f32[2,16,4,128]{3,2,1,0:T(4,128)S(1)}, u32[]{:S(2)}, u32[]{:S(2)}) %collective-permute-start.3) | collective-permute-done | bytes 65568 | tf_op jit(solution)/shard_map/ppermute | solution.py:18
  50.3 0.7 fusion.18
  51.0 0.6 fusion.101
  51.8 3.1 %collective-permute-start.4 = (f32[2,4,16,128]{3,2,1,0:T(8,128)S(1)}, f32[2,4,16,128]{3,2,1,0:T(8,128)S(1)}, u32[]{:S(2)}, u32[]{:S(2)}) collective-permute-start(f32[2,4,16,128]{3,2,1,0:T(8,128)S(1)} %get-tuple-element.33), channel_id=1, source_target_pairs={{4,0},{8,4},{12,8},{5,1},{9,5},{13,9},{6,2},{10,6},{14,10},{7,3},{... | collective-permute-start | bytes 196616 | tf_op jit(solution)/shard_map/ppermute | solution.py:20
  54.9 2.7 %collective-permute-start.5 = (f32[2,4,16,128]{3,2,1,0:T(8,128)S(1)}, f32[2,4,16,128]{3,2,1,0:T(8,128)S(1)}, u32[]{:S(2)}, u32[]{:S(2)}) collective-permute-start(f32[2,4,16,128]{3,2,1,0:T(8,128)S(1)} %get-tuple-element.32), channel_id=1, source_target_pairs={{0,4},{4,8},{8,12},{1,5},{5,9},{9,13},{2,6},{6,10},{10,14},{3,7},{... | collective-permute-start | bytes 196616 | tf_op jit(solution)/shard_map/ppermute | solution.py:18
  57.9 3.1 %collective-permute-done.5 = f32[2,4,16,128]{3,2,1,0:T(8,128)S(1)} collective-permute-done((f32[2,4,16,128]{3,2,1,0:T(8,128)S(1)}, f32[2,4,16,128]{3,2,1,0:T(8,128)S(1)}, u32[]{:S(2)}, u32[]{:S(2)}) %collective-permute-start.5) | collective-permute-done | bytes 65568 | tf_op jit(solution)/shard_map/ppermute | solution.py:18
  61.1 1.9 %collective-permute-start.6 = (f32[2,16,4,128]{3,2,1,0:T(4,128)S(1)}, f32[2,16,4,128]{3,2,1,0:T(4,128)S(1)}, u32[]{:S(2)}, u32[]{:S(2)}) collective-permute-start(f32[2,16,4,128]{3,2,1,0:T(4,128)S(1)} %get-tuple-element.23), channel_id=1, source_target_pairs={{1,0},{2,1},{3,2},{5,4},{6,5},{7,6},{9,8},{10,9},{11,10},{13,12},{... | collective-permute-start | bytes 196616 | tf_op jit(solution)/shard_map/ppermute | solution.py:20
  63.0 2.5 %collective-permute-start.7 = (f32[2,16,4,128]{3,2,1,0:T(4,128)S(1)}, f32[2,16,4,128]{3,2,1,0:T(4,128)S(1)}, u32[]{:S(2)}, u32[]{:S(2)}) collective-permute-start(f32[2,16,4,128]{3,2,1,0:T(4,128)S(1)} %get-tuple-element.22), channel_id=1, source_target_pairs={{0,1},{1,2},{2,3},{4,5},{5,6},{6,7},{8,9},{9,10},{10,11},{12,13},{... | collective-permute-start | bytes 196616 | tf_op jit(solution)/shard_map/ppermute | solution.py:18
  65.6 3.1 %collective-permute-done.7 = f32[2,16,4,128]{3,2,1,0:T(4,128)S(1)} collective-permute-done((f32[2,16,4,128]{3,2,1,0:T(4,128)S(1)}, f32[2,16,4,128]{3,2,1,0:T(4,128)S(1)}, u32[]{:S(2)}, u32[]{:S(2)}) %collective-permute-start.7) | collective-permute-done | bytes 65568 | tf_op jit(solution)/shard_map/ppermute | solution.py:18
  70.4 0.6 fusion.50
  71.0 0.7 fusion.155
  71.7 0.7 add_add_fusion
  (64 shorter events, 5.4 us)
Async XLA Ops:
  0.6 4.5 %copy-start = (f32[1024,128]{1,0:T(8,128)S(1)}, f32[1024,128]{1,0:T(8,128)}, u32[]{:S(2)}) copy-start(f32[1024,128]{1,0:T(8,128)} %param.24) | copy-start | bytes 1572868
  9.0 14.1 %all-to-all-start = ((f32[4,1,192]{2,1,0:T(1,128)}), f32[4,1,192]{2,1,0:T(1,128)S(1)}, u32[]{:S(2)}, u32[]{:S(2)}) async-start(f32[4,1,192]{2,1,0:T(1,128)} %reshape.120), calls=%async_computation | async-start | bytes 8192 | tf_op jit(solution)/shard_map/all_to_all | solution.py:138
  15.0 26.6 %collective-permute-start = (f32[2,4,16,128]{3,2,1,0:T(8,128)S(1)}, f32[2,4,16,128]{3,2,1,0:T(8,128)S(1)}, u32[]{:S(2)}, u32[]{:S(2)}) collective-permute-start(f32[2,4,16,128]{3,2,1,0:T(8,128)S(1)} %get-tuple-element.42), channel_id=1, source_target_pairs={{4,0},{8,4},{12,8},{5,1},{9,5},{13,9},{6,2},{10,6},{14,10},{7,3},{... | collective-permute-start | bytes 196616 | tf_op jit(solution)/shard_map/ppermute | solution.py:20
  17.5 24.1 %collective-permute-start.1 = (f32[2,4,16,128]{3,2,1,0:T(8,128)S(1)}, f32[2,4,16,128]{3,2,1,0:T(8,128)S(1)}, u32[]{:S(2)}, u32[]{:S(2)}) collective-permute-start(f32[2,4,16,128]{3,2,1,0:T(8,128)S(1)} %get-tuple-element.41), channel_id=1, source_target_pairs={{0,4},{4,8},{8,12},{1,5},{5,9},{9,13},{2,6},{6,10},{10,14},{3,7},{... | collective-permute-start | bytes 196616 | tf_op jit(solution)/shard_map/ppermute | solution.py:18
  29.3 12.3 %copy-start.1 = (f32[8,16,128]{2,1,0:T(8,128)S(1)}, f32[8,16,128]{2,1,0:T(8,128)}, u32[]{:S(2)}) copy-start(f32[8,16,128]{2,1,0:T(8,128)} %param.15) | copy-start | bytes 196612
  29.3 12.3 %copy-start.3 = (f32[8,16,128]{2,1,0:T(8,128)S(1)}, f32[8,16,128]{2,1,0:T(8,128)}, u32[]{:S(2)}) copy-start(f32[8,16,128]{2,1,0:T(8,128)} %param.14) | copy-start | bytes 196612
  41.7 4.6 %collective-permute-start.2 = (f32[2,16,4,128]{3,2,1,0:T(4,128)S(1)}, f32[2,16,4,128]{3,2,1,0:T(4,128)S(1)}, u32[]{:S(2)}, u32[]{:S(2)}) collective-permute-start(f32[2,16,4,128]{3,2,1,0:T(4,128)S(1)} %get-tuple-element.27), channel_id=1, source_target_pairs={{1,0},{2,1},{3,2},{5,4},{6,5},{7,6},{9,8},{10,9},{11,10},{13,12},{... | collective-permute-start | bytes 196616 | tf_op jit(solution)/shard_map/ppermute | solution.py:20
  43.6 7.9 %copy-start.5 = (f32[8,16,128]{2,1,0:T(8,128)S(1)}, f32[8,16,128]{2,1,0:T(8,128)}, u32[]{:S(2)}) copy-start(f32[8,16,128]{2,1,0:T(8,128)} %param.18) | copy-start | bytes 196612
  43.6 7.9 %copy-start.6 = (f32[8,16,128]{2,1,0:T(8,128)S(1)}, f32[8,16,128]{2,1,0:T(8,128)}, u32[]{:S(2)}) copy-start(f32[8,16,128]{2,1,0:T(8,128)} %param.20) | copy-start | bytes 196612
  43.7 7.9 %copy-start.8 = (f32[8,16,128]{2,1,0:T(8,128)S(1)}, f32[8,16,128]{2,1,0:T(8,128)}, u32[]{:S(2)}) copy-start(f32[8,16,128]{2,1,0:T(8,128)} %param.17) | copy-start | bytes 196612
  43.7 5.7 %collective-permute-start.3 = (f32[2,16,4,128]{3,2,1,0:T(4,128)S(1)}, f32[2,16,4,128]{3,2,1,0:T(4,128)S(1)}, u32[]{:S(2)}, u32[]{:S(2)}) collective-permute-start(f32[2,16,4,128]{3,2,1,0:T(4,128)S(1)} %get-tuple-element.26), channel_id=1, source_target_pairs={{0,1},{1,2},{2,3},{4,5},{5,6},{6,7},{8,9},{9,10},{10,11},{12,13},{... | collective-permute-start | bytes 196616 | tf_op jit(solution)/shard_map/ppermute | solution.py:18
  46.3 5.4 %copy-start.7 = (f32[8,16,128]{2,1,0:T(8,128)S(1)}, f32[8,16,128]{2,1,0:T(8,128)}, u32[]{:S(2)}) copy-start(f32[8,16,128]{2,1,0:T(8,128)} %param.19) | copy-start | bytes 196612
  46.3 5.4 %copy-start.9 = (f32[8,16,128]{2,1,0:T(8,128)S(1)}, f32[8,16,128]{2,1,0:T(8,128)}, u32[]{:S(2)}) copy-start(f32[8,16,128]{2,1,0:T(8,128)} %param.16) | copy-start | bytes 196612
  51.7 20.1 %copy-start.2 = (f32[8,16,128]{2,1,0:T(8,128)}, f32[8,16,128]{2,1,0:T(8,128)S(1)}, u32[]{:S(2)}) copy-start(f32[8,16,128]{2,1,0:T(8,128)S(1)} %get-tuple-element.14) | copy-start | bytes 196612
  51.8 19.2 %copy-start.4 = (f32[8,16,128]{2,1,0:T(8,128)}, f32[8,16,128]{2,1,0:T(8,128)S(1)}, u32[]{:S(2)}) copy-start(f32[8,16,128]{2,1,0:T(8,128)S(1)} %add_add_fusion.3) | copy-start | bytes 196612
  51.8 6.2 %collective-permute-start.4 = (f32[2,4,16,128]{3,2,1,0:T(8,128)S(1)}, f32[2,4,16,128]{3,2,1,0:T(8,128)S(1)}, u32[]{:S(2)}, u32[]{:S(2)}) collective-permute-start(f32[2,4,16,128]{3,2,1,0:T(8,128)S(1)} %get-tuple-element.33), channel_id=1, source_target_pairs={{4,0},{8,4},{12,8},{5,1},{9,5},{13,9},{6,2},{10,6},{14,10},{7,3},{... | collective-permute-start | bytes 196616 | tf_op jit(solution)/shard_map/ppermute | solution.py:20
  54.9 6.2 %collective-permute-start.5 = (f32[2,4,16,128]{3,2,1,0:T(8,128)S(1)}, f32[2,4,16,128]{3,2,1,0:T(8,128)S(1)}, u32[]{:S(2)}, u32[]{:S(2)}) collective-permute-start(f32[2,4,16,128]{3,2,1,0:T(8,128)S(1)} %get-tuple-element.32), channel_id=1, source_target_pairs={{0,4},{4,8},{8,12},{1,5},{5,9},{9,13},{2,6},{6,10},{10,14},{3,7},{... | collective-permute-start | bytes 196616 | tf_op jit(solution)/shard_map/ppermute | solution.py:18
  61.1 4.5 %collective-permute-start.6 = (f32[2,16,4,128]{3,2,1,0:T(4,128)S(1)}, f32[2,16,4,128]{3,2,1,0:T(4,128)S(1)}, u32[]{:S(2)}, u32[]{:S(2)}) collective-permute-start(f32[2,16,4,128]{3,2,1,0:T(4,128)S(1)} %get-tuple-element.23), channel_id=1, source_target_pairs={{1,0},{2,1},{3,2},{5,4},{6,5},{7,6},{9,8},{10,9},{11,10},{13,12},{... | collective-permute-start | bytes 196616 | tf_op jit(solution)/shard_map/ppermute | solution.py:20
  63.0 8.0 %copy-start.10 = (bf16[2,8,16,128]{3,2,1,0:T(8,128)(2,1)S(1)}, bf16[2,8,16,128]{3,2,1,0:T(8,128)(2,1)}, u32[]{:S(2)}) copy-start(bf16[2,8,16,128]{3,2,1,0:T(8,128)(2,1)} %param.23) | copy-start | bytes 196612
  63.0 5.7 %collective-permute-start.7 = (f32[2,16,4,128]{3,2,1,0:T(4,128)S(1)}, f32[2,16,4,128]{3,2,1,0:T(4,128)S(1)}, u32[]{:S(2)}, u32[]{:S(2)}) collective-permute-start(f32[2,16,4,128]{3,2,1,0:T(4,128)S(1)} %get-tuple-element.22), channel_id=1, source_target_pairs={{0,1},{1,2},{2,3},{4,5},{5,6},{6,7},{8,9},{9,10},{10,11},{12,13},{... | collective-permute-start | bytes 196616 | tf_op jit(solution)/shard_map/ppermute | solution.py:18
